TPU v7x, 32 devices: a whole 2x2x4 slice. The times are simulated.
32 devices in a mesh: cuts: 2 (over x), mode: 16 (over z, y, core).
Axes of the slice: x: 2, y: 2, z: 4, core: 2. Of those that a mesh axis runs over, the one named last changes fastest.
Arguments:
- stem_blocks: bfloat16 [2, 4096, 2, 256], P('cuts', 'mode'), may hold values from -6 to 6
- w1_table: bfloat16 [8, 2, 256, 256], replicated, may hold values from -0.25 to 0.25
- w2_table: bfloat16 [8, 2, 256, 256], replicated, may hold values from -0.125 to 0.125
- slice_ids: int32 [2, 2, 2], P('cuts'), may hold values from 0 to 7, as said below
- mode_perm: int32 [256], replicated, may hold values from 0 to 255, each once
Outputs:
- amplitudes: float32 [256, 16, 2, 256], P('mode', 'cuts')
Inputs may be any that keep to these rules, and one draw needn't show every extreme that they name: For each stem block b, the 2 values slice_ids[:,b,0] are distinct, and so are the 2 values slice_ids[:,b,1]. `mode_perm`: each column appears once.
All inputs are finite; a program needn't handle non-finite values.
Results may differ from a plain program's by a relative error of at most 0.0029.
Values may be sent and summed in bfloat16 or wider, within the bound.
No kernel may reach another device: no remote copies, remote signals or barrier semaphores. Data moves between devices by JAX's collectives and lax.ppermute only.
A program may use at most 64 MiB of HBM per device.

v0:
```python
import jax
import jax.numpy as jnp
from jax import lax
from jax.sharding import PartitionSpec as P


def broadcast(block, axis, source):
    block = jnp.where(lax.axis_index(axis) == source, block, jnp.zeros_like(block))
    return lax.psum(block, axis)


def widen_first(entry):
    real_part, imag_part = (entry[0], entry[1])
    upper = jnp.concatenate([real_part, imag_part], axis=1)
    lower = jnp.concatenate([-imag_part, real_part], axis=1)
    return jnp.concatenate([upper, lower], axis=0)


def widen_second(entry):
    real_part, imag_part = (entry[0], entry[1])
    first_row = jnp.concatenate([real_part, imag_part], axis=1)
    second_row = jnp.concatenate([-imag_part, real_part], axis=1)
    return jnp.stack([first_row, second_row], axis=0)


def second_step(exchanged, weight_two, contract_cols, free_cols):
    block_count, mode_count, piece_rows, _ = exchanged.shape
    pieces = exchanged.reshape(block_count, mode_count, piece_rows, 2, contract_cols, free_cols)
    wide_out = weight_two.shape[3]
    shaped = weight_two.reshape(block_count, 2, mode_count, contract_cols, wide_out)
    return jnp.einsum("nhqpcs,nphco->qso", pieces, shaped, preferred_element_type=jnp.float32)


def on_device(stem_blocks, w1_table, w2_table, slice_ids, mode_perm):
    mode_count = lax.axis_size("mode")
    row_count = stem_blocks.shape[1]
    stem_width = stem_blocks.shape[3]
    mid_width = w1_table.shape[3]
    inner_width = w2_table.shape[2]
    out_width = w2_table.shape[3]
    piece_rows = row_count // mode_count
    contract_cols = inner_width // mode_count
    free_cols = mid_width // contract_cols
    block_count = slice_ids.shape[1]
    first_all = jax.vmap(widen_first)(jnp.take(w1_table, mode_perm, axis=3))
    second_all = jax.vmap(widen_second)(w2_table)
    own_slices = slice_ids[0]
    begin = jnp.zeros((piece_rows, free_cols, 2 * out_width), jnp.float32)

    def one_block(block_index, running):
        stem_part = broadcast(stem_blocks[0], "cuts", block_index)
        slice_pair = own_slices[block_index]
        weight_one = lax.dynamic_index_in_dim(first_all, slice_pair[0], 0, keepdims=False)
        product = jnp.dot(
            stem_part.reshape(row_count, 2 * stem_width),
            weight_one,
            preferred_element_type=jnp.float32,
        ).astype(jnp.bfloat16)
        exchanged = lax.all_to_all(
            product[None, None], "mode", split_axis=2, concat_axis=1, tiled=True
        )
        weight_two = lax.dynamic_index_in_dim(second_all, slice_pair[1], 0, keepdims=True)
        return running + second_step(exchanged, weight_two, contract_cols, free_cols)

    amplitude = lax.fori_loop(0, block_count, one_block, begin)
    summed = lax.psum_scatter(amplitude, "cuts", scatter_dimension=1, tiled=True)
    return summed.reshape(piece_rows, summed.shape[1], 2, out_width)


def solution(mesh):
    placed = (P("cuts", "mode", None, None), P(), P(), P("cuts", None, None), P())
    return jax.shard_map(
        on_device,
        mesh=mesh,
        in_specs=placed,
        out_specs=P("mode", "cuts", None, None),
        check_vma=False,
    )
```

profile of v0, /device:TPU:0, one launch (start us, length us, event | category | flops | bytes accessed | tf_op | source)
XLA Modules:
  0.0 173.1 jit_solution(13787529332660151836)
XLA Ops:
  7.4 3.2 %slice_bitcast_fusion.2 = (bf16[8,256,256]{2,1,0:T(8,128)(2,1)}, bf16[8,256,256]{2,1,0:T(8,128)(2,1)}) fusion(bf16[8,2,256,256]{3,2,1,0:T(8,128)(2,1)} %param.9), kind=kLoop, calls=%fused_computation.19 | loop fusion | bytes 4194304 | tf_op jit(solution)/shard_map/vmap()/squeeze | solution.py:20
  10.6 1.1 fusion.6
  11.7 0.9 copy-done.6
  12.6 3.1 %copy.29 = bf16[8,2,256,256]{2,0,3,1:T(8,128)(2,1)} copy(bf16[8,2,256,256]{3,2,1,0:T(8,128)(2,1)S(1)} %copy-done.6) | data formatting | bytes 4194304 | tf_op args[1]
  15.7 2.4 %gather_fusion = bf16[256,8,2,256]{3,1,2,0:T(8,128)(2,1)S(1)} fusion(bf16[8,2,256,256]{2,0,3,1:T(8,128)(2,1)} %copy.29, s32[1024]{0:T(1024)S(1)} %pad_clamp_fusion), kind=kCustom, calls=%fused_computation | custom fusion | bytes 4195328 | tf_op jit(solution)/shard_map/jit(_take)/gather | solution.py:45
  18.1 0.9 select_bitcast_fusion
  19.0 1.1 slice_bitcast_fusion
  20.2 13.0 %maximum_maximum_fusion = bf16[8,512,512]{1,0,2:T(8,128)(2,1)} fusion(bf16[8,256,256]{1,0,2:T(8,128)(2,1)} %get-tuple-element.171, bf16[8,256,256]{1,0,2:T(8,128)(2,1)S(1)} %fusion.7, bf16[8,256,256]{1,0,2:T(8,128)(2,1)S(1)} %get-tuple-element.170), kind=kLoop, calls=%fused_computation.12 | loop fusion | flops 16777216 | bytes 7340032 | tf_op jit(solution)/shard_map/vmap()/concatenate | solution.py:16
  33.3 7.7 %copy.34 = bf16[8,512,512]{2,1,0:T(8,128)(2,1)} copy(bf16[8,512,512]{1,0,2:T(8,128)(2,1)} %maximum_maximum_fusion) | data formatting | bytes 8388608
  41.0 1.9 %maximum_bitcast_fusion.1 = (bf16[1,8,256,512]{3,2,0,1:T(8,128)(2,1)S(1)}, bf16[1,8,256,512]{3,2,0,1:T(8,128)(2,1)S(1)}) fusion(bf16[8,256,256]{2,1,0:T(8,128)(2,1)S(1)} %copy-done.5, bf16[8,256,256]{2,1,0:T(8,128)(2,1)} %get-tuple-element.169, bf16[8,256,256]{2,1,0:T(8,128)(2,1)S(1)} %copy-done.4), kind=kLoop, calls=%fused_computation.14 | loop fusion | flops 8388608 | bytes 7340032 | tf_op jit(solution)/shard_map/vmap()/stack | solution.py:23
  42.9 2.3 %maximum_bitcast_fusion = bf16[8,2,256,512]{3,2,1,0:T(8,128)(2,1)} fusion(bf16[1,8,256,512]{3,2,0,1:T(8,128)(2,1)S(1)} %get-tuple-element.173, bf16[1,8,256,512]{3,2,0,1:T(8,128)(2,1)S(1)} %get-tuple-element.172), kind=kLoop, calls=%fused_computation.13 | loop fusion | flops 2097152 | bytes 8388608 | tf_op jit(solution)/shard_map/vmap()/transpose | solution.py:46
  45.3 104.0 %while.14 = (s32[]{:T(128)}, f32[16,16,512]{2,1,0:T(8,128)S(1)}, bf16[1,256,2,256]{3,2,1,0:T(2,128)(2,1)S(1)}, s32[2,2]{1,0:T(2,128)S(1)}, bf16[8,512,512]{2,1,0...) while((s32[]{:T(128)}, f32[16,16,512]{2,1,0:T(8,128)S(1)}, ...), condition=%wide.region_2.3_spmd.clone, body=%wide.region_0.0_spmd.clone.sunk | while | flops 269090816 | bytes 11534731 | solution.py:65
  48.9 25.5 %all-reduce.2.cloned.1.call-done = bf16[256,512]{1,0:T(8,128)(2,1)} async-done(((bf16[256,512]{1,0:T(8,128)(2,1)}), bf16[256,512]{1,0:T(8,128)(2,1)}) %all-reduce.2.cloned.1.call-update) | async-done | bytes 262160 | tf_op jit(solution)/shard_map/while/body/eval_jaxpr/psum | solution.py:9
  74.4 1.4 fusion.23
  76.7 2.2 %reduce.6 = bf16[256,512]{1,0:T(8,128)(2,1)S(1)} reduce(bf16[256,1,1,512]{3,2,1,0:T(2,128)(2,1)S(1)} %bitcast.79, bf16[]{:T(256)} %broadcast.40), dimensions={1,2}, to_apply=%bitcast.54.reduce_sub_computation | reduce | bytes 524290 | tf_op jit(solution)/shard_map/while
  79.0 0.9 reshape.66
  79.8 5.6 %all-to-all-start = ((bf16[16,2,4096]{2,1,0:T(2,128)(2,1)}), bf16[16,2,4096]{2,1,0:T(2,128)(2,1)S(1)}, u32[]{:S(2)}, u32[]{:S(2)}) async-start(bf16[16,2,4096]{2,1,0:T(2,128)(2,1)} %reshape.66), calls=%async_computation | async-start | bytes 524288 | tf_op jit(solution)/shard_map/while/body/eval_jaxpr/all_to_all | solution.py:59
  87.5 1.1 constant_dynamic-slice_fusion.5
  88.6 6.9 %all-to-all-done = bf16[16,2,4096]{2,1,0:T(2,128)(2,1)S(1)} async-done(((bf16[16,2,4096]{2,1,0:T(2,128)(2,1)}), bf16[16,2,4096]{2,1,0:T(2,128)(2,1)S(1)}, u32[]{:S(2)}, u32[]{:S(2)}) %all-to-all-start) | async-done | bytes 262176 | tf_op jit(solution)/shard_map/while/body/eval_jaxpr/all_to_all | solution.py:59
  95.8 1.5 bitcast_reduce_fusion.2
  97.3 1.7 reshape.68
  103.5 20.2 %all-reduce.2.cloned.1.call-done = bf16[256,512]{1,0:T(8,128)(2,1)} async-done(((bf16[256,512]{1,0:T(8,128)(2,1)}), bf16[256,512]{1,0:T(8,128)(2,1)}) %all-reduce.2.cloned.1.call-update) | async-done | bytes 262160 | tf_op jit(solution)/shard_map/while/body/eval_jaxpr/psum | solution.py:9
  123.7 1.4 fusion.23
  126.1 2.2 %reduce.6 = bf16[256,512]{1,0:T(8,128)(2,1)S(1)} reduce(bf16[256,1,1,512]{3,2,1,0:T(2,128)(2,1)S(1)} %bitcast.79, bf16[]{:T(256)} %broadcast.40), dimensions={1,2}, to_apply=%bitcast.54.reduce_sub_computation | reduce | bytes 524290 | tf_op jit(solution)/shard_map/while
  128.3 0.9 reshape.66
  129.2 5.6 %all-to-all-start = ((bf16[16,2,4096]{2,1,0:T(2,128)(2,1)}), bf16[16,2,4096]{2,1,0:T(2,128)(2,1)S(1)}, u32[]{:S(2)}, u32[]{:S(2)}) async-start(bf16[16,2,4096]{2,1,0:T(2,128)(2,1)} %reshape.66), calls=%async_computation | async-start | bytes 524288 | tf_op jit(solution)/shard_map/while/body/eval_jaxpr/all_to_all | solution.py:59
  136.9 1.1 constant_dynamic-slice_fusion.5
  138.0 6.9 %all-to-all-done = bf16[16,2,4096]{2,1,0:T(2,128)(2,1)S(1)} async-done(((bf16[16,2,4096]{2,1,0:T(2,128)(2,1)}), bf16[16,2,4096]{2,1,0:T(2,128)(2,1)S(1)}, u32[]{:S(2)}, u32[]{:S(2)}) %all-to-all-start) | async-done | bytes 262176 | tf_op jit(solution)/shard_map/while/body/eval_jaxpr/all_to_all | solution.py:59
  145.1 1.5 bitcast_reduce_fusion.2
  146.6 1.7 reshape.68
  150.1 13.7 %reduce-scatter.2.cloned.1.call-done = f32[16,8,512]{2,1,0:T(8,128)} async-done(((f32[16,16,512]{2,1,0:T(8,128)}), f32[16,8,512]{2,1,0:T(8,128)}) %reduce-scatter.2.cloned.1.call-update) | async-done | bytes 262160 | tf_op jit(solution)/shard_map/reduce_scatter | solution.py:66
  163.8 1.8 %reshape.44 = f32[16,8,2,256]{3,2,1,0:T(2,128)} reshape(f32[16,8,512]{2,1,0:T(8,128)} %reduce-scatter.2.cloned.1.call-done) | data formatting | bytes 524288 | tf_op jit(solution)/shard_map/reshape | solution.py:67
  (46 shorter events, 8.5 us)
Async XLA Ops:
  7.4 3.2 %copy-start.3 = (bf16[8,2,256,256]{3,2,1,0:T(8,128)(2,1)S(1)}, bf16[8,2,256,256]{3,2,1,0:T(8,128)(2,1)}, u32[]{:S(2)}) copy-start(bf16[8,2,256,256]{3,2,1,0:T(8,128)(2,1)} %param.9) | copy-start | bytes 6291460
  7.4 4.3 %copy-start.7 = (s32[256]{0:T(256)S(1)}, s32[256]{0:T(256)}, u32[]{:S(2)}) copy-start(s32[256]{0:T(256)} %param.11) | copy-start | bytes 3076
  10.6 2.0 %copy-start.6 = (bf16[8,2,256,256]{3,2,1,0:T(8,128)(2,1)S(1)}, bf16[8,2,256,256]{3,2,1,0:T(8,128)(2,1)}, u32[]{:S(2)}) copy-start(bf16[8,2,256,256]{3,2,1,0:T(8,128)(2,1)} %param.8) | copy-start | bytes 6291460
  33.3 7.7 %copy-start.4 = (bf16[8,256,256]{2,1,0:T(8,128)(2,1)S(1)}, bf16[8,256,256]{2,1,0:T(8,128)(2,1)}, u32[]{:S(2)}) copy-start(bf16[8,256,256]{2,1,0:T(8,128)(2,1)} %fusion.6) | copy-start | bytes 3145732
  33.3 7.7 %copy-start.5 = (bf16[8,256,256]{2,1,0:T(8,128)(2,1)S(1)}, bf16[8,256,256]{2,1,0:T(8,128)(2,1)}, u32[]{:S(2)}) copy-start(bf16[8,256,256]{2,1,0:T(8,128)(2,1)} %get-tuple-element.168) | copy-start | bytes 3145732
  42.9 2.4 %copy-start.1 = (bf16[1,256,2,256]{3,2,1,0:T(2,128)(2,1)S(1)}, bf16[1,256,2,256]{3,2,1,0:T(2,128)(2,1)}, u32[]{:S(2)}) copy-start(bf16[1,256,2,256]{3,2,1,0:T(2,128)(2,1)} %param.7) | copy-start | bytes 786436
  42.9 2.4 %copy-start.8 = (s32[1,2,2]{2,1,0:T(2,128)S(1)}, s32[1,2,2]{2,1,0:T(2,128)}, u32[]{:S(2)}) copy-start(s32[1,2,2]{2,1,0:T(2,128)} %param.10) | copy-start | bytes 52
  45.3 29.1 %all-reduce.2.cloned.1.call-start = ((), (), s32[]{:S(2)}) async-start(), calls=%async_computation.3 | async-start | bytes 524288 | tf_op jit(solution)/shard_map/while/body/eval_jaxpr/psum | solution.py:9
  79.8 15.7 %all-to-all-start = ((bf16[16,2,4096]{2,1,0:T(2,128)(2,1)}), bf16[16,2,4096]{2,1,0:T(2,128)(2,1)S(1)}, u32[]{:S(2)}, u32[]{:S(2)}) async-start(bf16[16,2,4096]{2,1,0:T(2,128)(2,1)} %reshape.66), calls=%async_computation | async-start | bytes 524288 | tf_op jit(solution)/shard_map/while/body/eval_jaxpr/all_to_all | solution.py:59
  99.0 1.0 copy-start.2
  99.9 23.8 %all-reduce.2.cloned.1.call-start = ((), (), s32[]{:S(2)}) async-start(), calls=%async_computation.3 | async-start | bytes 524288 | tf_op jit(solution)/shard_map/while/body/eval_jaxpr/psum | solution.py:9
  129.2 15.7 %all-to-all-start = ((bf16[16,2,4096]{2,1,0:T(2,128)(2,1)}), bf16[16,2,4096]{2,1,0:T(2,128)(2,1)S(1)}, u32[]{:S(2)}, u32[]{:S(2)}) async-start(bf16[16,2,4096]{2,1,0:T(2,128)(2,1)} %reshape.66), calls=%async_computation | async-start | bytes 524288 | tf_op jit(solution)/shard_map/while/body/eval_jaxpr/all_to_all | solution.py:59
  148.3 1.0 copy-start.2
  149.3 0.8 copy-start
  149.3 14.5 %reduce-scatter.2.cloned.1.call-start = ((), (), s32[]{:S(2)}) async-start(), calls=%async_computation.2 | async-start | bytes 786432 | tf_op jit(solution)/shard_map/reduce_scatter | solution.py:66
Sparse Core Ops, SparseCore 0:
  48.5 25.8 all-reduce.1
  103.1 20.5 all-reduce.1
Sparse Core Ops, SparseCore 1:
  152.0 11.8 reduce-scatter.1
where the time goes:
time: 174 us; the launch traced here: 173 us
  waiting for transfers between devices  73.3 us (42%)
  local copies, waits for them, and re-layouts  37 us (21%)
  other arithmetic  24.2 us (14%)
  between operations  14.9 us (9%)
  starting transfers between devices  11.3 us (6%)
  loops' own time  8.19 us (5%)
  matrix products  4.28 us (2%)
    psum x2, waiting for transfers between devices, broadcast(): return lax.psum(block, axis)  45.7 us
    all_to_all x2, waiting for transfers between devices, one_block(): lax.all_to_all(product[None, None], 'mode', split_axis=2, concat_axis=1,...  13.8 us
    reduce_scatter x1, waiting for transfers between devices, on_device(): lax.psum_scatter(amplitude, 'cuts', scatter_dimension=1, tiled=True)  13.7 us
    concatenate x1, other arithmetic, widen_first(): return jnp.concatenate([upper, lower], axis=0)  13 us
    unnamed x18, local copies, waits for them, and re-layouts  12.5 us
    all_to_all x2, starting transfers between devices, one_block(): lax.all_to_all(product[None, None], 'mode', split_axis=2, concat_axis=1,...  11.2 us
    another operation x1, loops' own time, on_device(): amplitude = lax.fori_loop(0, block_count, one_block, begin)  8.19 us
    while x12, local copies, waits for them, and re-layouts  5.23 us
  transfers between devices with their start and end apart: 5, of which 5 were waited for; matrix products, arithmetic and copies ran while one was open for 2% of the time, Pallas kernels for 0%

commit v1 on v0

--- a/solution.py
+++ b/solution.py
@@ -1,7 +1,32 @@
+import functools
 import jax
 import jax.numpy as jnp
 from jax import lax
 from jax.sharding import PartitionSpec as P
+
+
+def list_the_marks(sheet, on_dim, in_dim):
+    top = jax.lax.axis_size("mode")
+    res = jax.lax.axis_index("mode")
+    d_next, v_next = (top, res)
+    plain = sheet.shape[in_dim] // d_next
+    w2 = list(sheet.shape)
+    w2[in_dim] = plain
+    current_block = w2[on_dim]
+    w2[on_dim] = current_block * d_next
+    frame_out = jnp.zeros(w2, sheet.dtype)
+    for tick in range(d_next):
+        h_now = lax.dynamic_slice_in_dim(sheet, (v_next ^ tick) * plain, plain, axis=in_dim)
+        if tick:
+            newest = tuple(((t, t ^ tick) for t in range(d_next)))
+            h_now = jax.lax.ppermute(h_now, axis_name="mode", perm=newest)
+        frame_out = lax.dynamic_update_slice_in_dim(
+            frame_out, h_now, (v_next ^ tick) * current_block, axis=on_dim
+        )
+    return frame_out
+
+
+open_the_pools = functools.partial(list_the_marks, on_dim=1, in_dim=2)
 
 
 def broadcast(block, axis, source):
@@ -56,9 +81,7 @@
             weight_one,
             preferred_element_type=jnp.float32,
         ).astype(jnp.bfloat16)
-        exchanged = lax.all_to_all(
-            product[None, None], "mode", split_axis=2, concat_axis=1, tiled=True
-        )
+        exchanged = open_the_pools(product[None, None])
         weight_two = lax.dynamic_index_in_dim(second_all, slice_pair[1], 0, keepdims=True)
         return running + second_step(exchanged, weight_two, contract_cols, free_cols)
 

time: 174 us -> 182 us (1.046)
  starting transfers between devices: 11.3 us -> 41.2 us
  waiting for transfers between devices: 73.3 us -> 62.1 us
  local copies, waits for them, and re-layouts: 37 us -> 29.7 us
  other arithmetic: 24.2 us -> 20.9 us
    ppermute x0 -> x30, starting transfers between devices: none -> 41.1 us  [list_the_marks(): h_now = jax.lax.ppermute(h_now, axis_name='mode', perm=newest)]
    all_to_all x2 -> x0, waiting for transfers between devices: 13.8 us -> none  [one_block(): lax.all_to_all(product[None, None], 'mode', split_axis=2, concat_axis=1,...]
    all_to_all x2 -> x0, starting transfers between devices: 11.2 us -> none  [one_block(): lax.all_to_all(product[None, None], 'mode', split_axis=2, concat_axis=1,...]
    ppermute x0 -> x30, waiting for transfers between devices: none -> 11.2 us  [list_the_marks(): h_now = jax.lax.ppermute(h_now, axis_name='mode', perm=newest)]
    psum x2, waiting for transfers between devices: 45.7 us -> 38.1 us  [broadcast(): return lax.psum(block, axis)]
    while x2 -> x0, other arithmetic: 4.41 us -> none
    while x12 -> x2, local copies, waits for them, and re-layouts: 5.23 us -> 1.47 us
    all_to_all x2 -> x0, local copies, waits for them, and re-layouts: 2.98 us -> none  [one_block(): lax.all_to_all(product[None, None], 'mode', split_axis=2, concat_axis=1,...]
  transfers between devices with their start and end apart: 5 -> 33, of which waited for: 5 -> 9; matrix products, arithmetic and copies ran while one was open for 2% -> 2% of each run, Pallas kernels for 0% -> 0%
where the time goes in v1:
time: 182 us; the launch traced here: 181 us
  waiting for transfers between devices  62.1 us (34%)
  starting transfers between devices  41.2 us (23%)
  local copies, waits for them, and re-layouts  29.7 us (16%)
  other arithmetic  20.9 us (11%)
  between operations  14.9 us (8%)
  loops' own time  7.82 us (4%)
  matrix products  4.28 us (2%)
    ppermute x30, starting transfers between devices, list_the_marks(): h_now = jax.lax.ppermute(h_now, axis_name='mode', perm=newest)  41.1 us
    psum x2, waiting for transfers between devices, broadcast(): return lax.psum(block, axis)  38.1 us
    concatenate x1, other arithmetic, widen_first(): return jnp.concatenate([upper, lower], axis=0)  13.1 us
    reduce_scatter x1, waiting for transfers between devices, on_device(): lax.psum_scatter(amplitude, 'cuts', scatter_dimension=1, tiled=True)  12.8 us
    unnamed x16, local copies, waits for them, and re-layouts  12.6 us
    ppermute x30, waiting for transfers between devices, list_the_marks(): h_now = jax.lax.ppermute(h_now, axis_name='mode', perm=newest)  11.2 us
    another operation x1, loops' own time, on_device(): amplitude = lax.fori_loop(0, block_count, one_block, begin)  7.82 us
  transfers between devices with their start and end apart: 33, of which 9 were waited for; matrix products, arithmetic and copies ran while one was open for 2% of the time, Pallas kernels for 0%

profile of v1, /device:TPU:0, one launch (start us, length us, event | category | flops | bytes accessed | tf_op | source)
XLA Modules:
  0.0 181.0 jit_solution(16949929105906179372)
XLA Ops:
  7.4 3.3 %slice_bitcast_fusion.2 = (bf16[8,256,256]{2,1,0:T(8,128)(2,1)}, bf16[8,256,256]{2,1,0:T(8,128)(2,1)}) fusion(bf16[8,2,256,256]{3,2,1,0:T(8,128)(2,1)} %param.9), kind=kLoop, calls=%fused_computation.49 | loop fusion | bytes 4194304 | tf_op jit(solution)/shard_map/vmap()/squeeze | solution.py:45
  12.6 3.1 %copy.11 = bf16[8,2,256,256]{2,0,3,1:T(8,128)(2,1)} copy(bf16[8,2,256,256]{3,2,1,0:T(8,128)(2,1)S(1)} %copy-done.4) | data formatting | bytes 4194304 | tf_op args[1]
  15.7 2.4 %gather_fusion = bf16[256,8,2,256]{3,1,2,0:T(8,128)(2,1)S(1)} fusion(bf16[8,2,256,256]{2,0,3,1:T(8,128)(2,1)} %copy.11, s32[1024]{0:T(1024)S(1)} %pad_clamp_fusion), kind=kCustom, calls=%fused_computation | custom fusion | bytes 4195328 | tf_op jit(solution)/shard_map/jit(_take)/gather | solution.py:70
  20.3 13.1 %maximum_maximum_fusion = bf16[8,512,512]{1,0,2:T(8,128)(2,1)} fusion(bf16[8,256,256]{1,0,2:T(8,128)(2,1)} %get-tuple-element.174, bf16[8,256,256]{1,0,2:T(8,128)(2,1)S(1)} %fusion.6, bf16[8,256,256]{1,0,2:T(8,128)(2,1)S(1)} %get-tuple-element.173), kind=kLoop, calls=%fused_computation.42 | loop fusion | flops 16777216 | bytes 7340032 | tf_op jit(solution)/shard_map/vmap()/concatenate | solution.py:41
  33.4 7.8 %copy.16 = bf16[8,512,512]{2,1,0:T(8,128)(2,1)} copy(bf16[8,512,512]{1,0,2:T(8,128)(2,1)} %maximum_maximum_fusion) | data formatting | bytes 8388608
  41.2 2.0 %maximum_bitcast_fusion.1 = (bf16[1,8,256,512]{3,2,0,1:T(8,128)(2,1)S(1)}, bf16[1,8,256,512]{3,2,0,1:T(8,128)(2,1)S(1)}) fusion(bf16[8,256,256]{2,1,0:T(8,128)(2,1)S(1)} %copy-done.3, bf16[8,256,256]{2,1,0:T(8,128)(2,1)} %get-tuple-element.172, bf16[8,256,256]{2,1,0:T(8,128)(2,1)S(1)} %copy-done.2), kind=kLoop, calls=%fused_computation.44 | loop fusion | flops 8388608 | bytes 7340032 | tf_op jit(solution)/shard_map/vmap()/stack | solution.py:48
  43.2 2.4 %maximum_bitcast_fusion = bf16[8,2,256,512]{3,2,1,0:T(8,128)(2,1)} fusion(bf16[1,8,256,512]{3,2,0,1:T(8,128)(2,1)S(1)} %get-tuple-element.176, bf16[1,8,256,512]{3,2,0,1:T(8,128)(2,1)S(1)} %get-tuple-element.175), kind=kLoop, calls=%fused_computation.43 | loop fusion | flops 2097152 | bytes 8388608 | tf_op jit(solution)/shard_map/vmap()/transpose | solution.py:71
  45.6 112.5 %while.14 = (s32[]{:T(128)}, f32[16,16,512]{2,1,0:T(8,128)S(1)}, bf16[1,256,2,256]{3,2,1,0:T(2,128)(2,1)}, s32[2,2]{1,0:T(2,128)S(1)}, bf16[8,512,512]{2,1,0:T(8...) while((s32[]{:T(128)}, f32[16,16,512]{2,1,0:T(8,128)S(1)}, ...), condition=%wide.region_2.3_spmd.clone, body=%wide.region_0.0_spmd.clone.sunk | while | flops 269090816 | bytes 9341539 | solution.py:88
  53.0 21.7 %all-reduce.2.cloned.1.call-done = bf16[256,512]{1,0:T(8,128)(2,1)} async-done(((bf16[256,512]{1,0:T(8,128)(2,1)}), bf16[256,512]{1,0:T(8,128)(2,1)}) %all-reduce.2.cloned.1.call-update) | async-done | bytes 262160 | tf_op jit(solution)/shard_map/while/body/eval_jaxpr/psum | solution.py:34
  76.3 1.5 collective-permute-start.1
  78.2 1.5 collective-permute-start.3
  79.9 2.5 %collective-permute-start.5 = (bf16[1,1,16,512]{3,2,1,0:T(8,128)(2,1)S(1)}, bf16[1,1,16,512]{3,2,1,0:T(8,128)(2,1)S(1)}, u32[]{:S(2)}, u32[]{:S(2)}) collective-permute-start(bf16[1,1,16,512]{3,2,1,0:T(8,128)(2,1)S(1)} %get-tuple-element.237), channel_id=1, source_target_pairs={{0,6},{1,7},{2,4},{3,5},{4,2},{5,3},{6,0},{7,1},{8,14},{9,15},{10,... | collective-permute-start | bytes 49160 | tf_op jit(solution)/shard_map/while/body/eval_jaxpr/ppermute | solution.py:22
  82.7 2.4 %collective-permute-start.7 = (bf16[1,1,16,512]{3,2,1,0:T(8,128)(2,1)S(1)}, bf16[1,1,16,512]{3,2,1,0:T(8,128)(2,1)S(1)}, u32[]{:S(2)}, u32[]{:S(2)}) collective-permute-start(bf16[1,1,16,512]{3,2,1,0:T(8,128)(2,1)S(1)} %get-tuple-element.239), channel_id=1, source_target_pairs={{0,8},{1,9},{2,10},{3,11},{4,12},{5,13},{6,14},{7,15},{8,0},{9,1},... | collective-permute-start | bytes 49160 | tf_op jit(solution)/shard_map/while/body/eval_jaxpr/ppermute | solution.py:22
  85.3 3.3 %collective-permute-start.9 = (bf16[1,1,16,512]{3,2,1,0:T(8,128)(2,1)S(1)}, bf16[1,1,16,512]{3,2,1,0:T(8,128)(2,1)S(1)}, u32[]{:S(2)}, u32[]{:S(2)}) collective-permute-start(bf16[1,1,16,512]{3,2,1,0:T(8,128)(2,1)S(1)} %get-tuple-element.241), channel_id=1, source_target_pairs={{0,10},{1,11},{2,8},{3,9},{4,14},{5,15},{6,12},{7,13},{8,2},{9,3},... | collective-permute-start | bytes 49160 | tf_op jit(solution)/shard_map/while/body/eval_jaxpr/ppermute | solution.py:22
  88.9 3.3 %collective-permute-start.11 = (bf16[1,1,16,512]{3,2,1,0:T(8,128)(2,1)S(1)}, bf16[1,1,16,512]{3,2,1,0:T(8,128)(2,1)S(1)}, u32[]{:S(2)}, u32[]{:S(2)}) collective-permute-start(bf16[1,1,16,512]{3,2,1,0:T(8,128)(2,1)S(1)} %get-tuple-element.243), channel_id=1, source_target_pairs={{0,12},{1,13},{2,14},{3,15},{4,8},{5,9},{6,10},{7,11},{8,4},{9,5},... | collective-permute-start | bytes 49160 | tf_op jit(solution)/shard_map/while/body/eval_jaxpr/ppermute | solution.py:22
  92.4 4.2 %collective-permute-start.13 = (bf16[1,1,16,512]{3,2,1,0:T(8,128)(2,1)S(1)}, bf16[1,1,16,512]{3,2,1,0:T(8,128)(2,1)S(1)}, u32[]{:S(2)}, u32[]{:S(2)}) collective-permute-start(bf16[1,1,16,512]{3,2,1,0:T(8,128)(2,1)S(1)} %get-tuple-element.245), channel_id=1, source_target_pairs={{0,14},{1,15},{2,12},{3,13},{4,10},{5,11},{6,8},{7,9},{8,6},{9,7},... | collective-permute-start | bytes 49160 | tf_op jit(solution)/shard_map/while/body/eval_jaxpr/ppermute | solution.py:22
  97.3 1.6 collective-permute-done.13
  98.8 3.7 %collective-permute-done.14 = bf16[1,1,16,512]{3,2,1,0:T(8,128)(2,1)S(1)} collective-permute-done((bf16[1,1,16,512]{3,2,1,0:T(8,128)(2,1)S(1)}, bf16[1,1,16,512]{3,2,1,0:T(8,128)(2,1)S(1)}, u32[]{:S(2)}, u32[]{:S(2)}) %collective-permute-start.14) | collective-permute-done | bytes 16416 | tf_op jit(solution)/shard_map/while/body/eval_jaxpr/ppermute | solution.py:22
  102.5 1.7 reshape.105
  111.5 16.4 %all-reduce.2.cloned.1.call-done = bf16[256,512]{1,0:T(8,128)(2,1)} async-done(((bf16[256,512]{1,0:T(8,128)(2,1)}), bf16[256,512]{1,0:T(8,128)(2,1)}) %all-reduce.2.cloned.1.call-update) | async-done | bytes 262160 | tf_op jit(solution)/shard_map/while/body/eval_jaxpr/psum | solution.py:34
  129.4 1.5 collective-permute-start.1
  131.3 1.5 collective-permute-start.3
  133.0 2.5 %collective-permute-start.5 = (bf16[1,1,16,512]{3,2,1,0:T(8,128)(2,1)S(1)}, bf16[1,1,16,512]{3,2,1,0:T(8,128)(2,1)S(1)}, u32[]{:S(2)}, u32[]{:S(2)}) collective-permute-start(bf16[1,1,16,512]{3,2,1,0:T(8,128)(2,1)S(1)} %get-tuple-element.237), channel_id=1, source_target_pairs={{0,6},{1,7},{2,4},{3,5},{4,2},{5,3},{6,0},{7,1},{8,14},{9,15},{10,... | collective-permute-start | bytes 49160 | tf_op jit(solution)/shard_map/while/body/eval_jaxpr/ppermute | solution.py:22
  135.8 2.4 %collective-permute-start.7 = (bf16[1,1,16,512]{3,2,1,0:T(8,128)(2,1)S(1)}, bf16[1,1,16,512]{3,2,1,0:T(8,128)(2,1)S(1)}, u32[]{:S(2)}, u32[]{:S(2)}) collective-permute-start(bf16[1,1,16,512]{3,2,1,0:T(8,128)(2,1)S(1)} %get-tuple-element.239), channel_id=1, source_target_pairs={{0,8},{1,9},{2,10},{3,11},{4,12},{5,13},{6,14},{7,15},{8,0},{9,1},... | collective-permute-start | bytes 49160 | tf_op jit(solution)/shard_map/while/body/eval_jaxpr/ppermute | solution.py:22
  138.4 3.3 %collective-permute-start.9 = (bf16[1,1,16,512]{3,2,1,0:T(8,128)(2,1)S(1)}, bf16[1,1,16,512]{3,2,1,0:T(8,128)(2,1)S(1)}, u32[]{:S(2)}, u32[]{:S(2)}) collective-permute-start(bf16[1,1,16,512]{3,2,1,0:T(8,128)(2,1)S(1)} %get-tuple-element.241), channel_id=1, source_target_pairs={{0,10},{1,11},{2,8},{3,9},{4,14},{5,15},{6,12},{7,13},{8,2},{9,3},... | collective-permute-start | bytes 49160 | tf_op jit(solution)/shard_map/while/body/eval_jaxpr/ppermute | solution.py:22
  142.0 3.3 %collective-permute-start.11 = (bf16[1,1,16,512]{3,2,1,0:T(8,128)(2,1)S(1)}, bf16[1,1,16,512]{3,2,1,0:T(8,128)(2,1)S(1)}, u32[]{:S(2)}, u32[]{:S(2)}) collective-permute-start(bf16[1,1,16,512]{3,2,1,0:T(8,128)(2,1)S(1)} %get-tuple-element.243), channel_id=1, source_target_pairs={{0,12},{1,13},{2,14},{3,15},{4,8},{5,9},{6,10},{7,11},{8,4},{9,5},... | collective-permute-start | bytes 49160 | tf_op jit(solution)/shard_map/while/body/eval_jaxpr/ppermute | solution.py:22
  145.5 4.2 %collective-permute-start.13 = (bf16[1,1,16,512]{3,2,1,0:T(8,128)(2,1)S(1)}, bf16[1,1,16,512]{3,2,1,0:T(8,128)(2,1)S(1)}, u32[]{:S(2)}, u32[]{:S(2)}) collective-permute-start(bf16[1,1,16,512]{3,2,1,0:T(8,128)(2,1)S(1)} %get-tuple-element.245), channel_id=1, source_target_pairs={{0,14},{1,15},{2,12},{3,13},{4,10},{5,11},{6,8},{7,9},{8,6},{9,7},... | collective-permute-start | bytes 49160 | tf_op jit(solution)/shard_map/while/body/eval_jaxpr/ppermute | solution.py:22
  150.4 1.6 collective-permute-done.13
  152.0 3.7 %collective-permute-done.14 = bf16[1,1,16,512]{3,2,1,0:T(8,128)(2,1)S(1)} collective-permute-done((bf16[1,1,16,512]{3,2,1,0:T(8,128)(2,1)S(1)}, bf16[1,1,16,512]{3,2,1,0:T(8,128)(2,1)S(1)}, u32[]{:S(2)}, u32[]{:S(2)}) %collective-permute-start.14) | collective-permute-done | bytes 16416 | tf_op jit(solution)/shard_map/while/body/eval_jaxpr/ppermute | solution.py:22
  155.6 1.7 reshape.105
  158.9 12.8 %reduce-scatter.2.cloned.1.call-done = f32[16,8,512]{2,1,0:T(8,128)} async-done(((f32[16,16,512]{2,1,0:T(8,128)}), f32[16,8,512]{2,1,0:T(8,128)}) %reduce-scatter.2.cloned.1.call-update) | async-done | bytes 262160 | tf_op jit(solution)/shard_map/reduce_scatter | solution.py:89
  171.7 1.8 %reshape.88 = f32[16,8,2,256]{3,2,1,0:T(2,128)} reshape(f32[16,8,512]{2,1,0:T(8,128)} %reduce-scatter.2.cloned.1.call-done) | data formatting | bytes 524288 | tf_op jit(solution)/shard_map/reshape | solution.py:90
  (120 shorter events, 20.2 us)
Async XLA Ops:
  45.6 29.1 %all-reduce.2.cloned.1.call-start = ((), (), s32[]{:S(2)}) async-start(), calls=%async_computation.2 | async-start | bytes 524288 | tf_op jit(solution)/shard_map/while/body/eval_jaxpr/psum | solution.py:34
  76.2 3.7 %collective-permute-start = (bf16[1,1,16,512]{3,2,1,0:T(8,128)(2,1)S(1)}, bf16[1,1,16,512]{3,2,1,0:T(8,128)(2,1)S(1)}, u32[]{:S(2)}, u32[]{:S(2)}) collective-permute-start(bf16[1,1,16,512]{3,2,1,0:T(8,128)(2,1)S(1)} %get-tuple-element.232), channel_id=1, source_target_pairs={{0,1},{1,0},{2,3},{3,2},{4,5},{5,4},{6,7},{7,6},{8,9},{9,8},{10,11... | collective-permute-start | bytes 49160 | tf_op jit(solution)/shard_map/while/body/eval_jaxpr/ppermute | solution.py:22
  76.3 6.1 %collective-permute-start.1 = (bf16[1,1,16,512]{3,2,1,0:T(8,128)(2,1)S(1)}, bf16[1,1,16,512]{3,2,1,0:T(8,128)(2,1)S(1)}, u32[]{:S(2)}, u32[]{:S(2)}) collective-permute-start(bf16[1,1,16,512]{3,2,1,0:T(8,128)(2,1)S(1)} %get-tuple-element.233), channel_id=1, source_target_pairs={{0,2},{1,3},{2,0},{3,1},{4,6},{5,7},{6,4},{7,5},{8,10},{9,11},{10,... | collective-permute-start | bytes 49160 | tf_op jit(solution)/shard_map/while/body/eval_jaxpr/ppermute | solution.py:22
  77.8 4.9 %collective-permute-start.2 = (bf16[1,1,16,512]{3,2,1,0:T(8,128)(2,1)S(1)}, bf16[1,1,16,512]{3,2,1,0:T(8,128)(2,1)S(1)}, u32[]{:S(2)}, u32[]{:S(2)}) collective-permute-start(bf16[1,1,16,512]{3,2,1,0:T(8,128)(2,1)S(1)} %get-tuple-element.234), channel_id=1, source_target_pairs={{0,3},{1,2},{2,1},{3,0},{4,7},{5,6},{6,5},{7,4},{8,11},{9,10},{10,... | collective-permute-start | bytes 49160 | tf_op jit(solution)/shard_map/while/body/eval_jaxpr/ppermute | solution.py:22
  78.2 6.9 %collective-permute-start.3 = (bf16[1,1,16,512]{3,2,1,0:T(8,128)(2,1)S(1)}, bf16[1,1,16,512]{3,2,1,0:T(8,128)(2,1)S(1)}, u32[]{:S(2)}, u32[]{:S(2)}) collective-permute-start(bf16[1,1,16,512]{3,2,1,0:T(8,128)(2,1)S(1)} %get-tuple-element.235), channel_id=1, source_target_pairs={{0,4},{1,5},{2,6},{3,7},{4,0},{5,1},{6,2},{7,3},{8,12},{9,13},{10,... | collective-permute-start | bytes 49160 | tf_op jit(solution)/shard_map/while/body/eval_jaxpr/ppermute | solution.py:22
  79.6 5.7 %collective-permute-start.4 = (bf16[1,1,16,512]{3,2,1,0:T(8,128)(2,1)S(1)}, bf16[1,1,16,512]{3,2,1,0:T(8,128)(2,1)S(1)}, u32[]{:S(2)}, u32[]{:S(2)}) collective-permute-start(bf16[1,1,16,512]{3,2,1,0:T(8,128)(2,1)S(1)} %get-tuple-element.236), channel_id=1, source_target_pairs={{0,5},{1,4},{2,7},{3,6},{4,1},{5,0},{6,3},{7,2},{8,13},{9,12},{10,... | collective-permute-start | bytes 49160 | tf_op jit(solution)/shard_map/while/body/eval_jaxpr/ppermute | solution.py:22
  79.9 8.7 %collective-permute-start.5 = (bf16[1,1,16,512]{3,2,1,0:T(8,128)(2,1)S(1)}, bf16[1,1,16,512]{3,2,1,0:T(8,128)(2,1)S(1)}, u32[]{:S(2)}, u32[]{:S(2)}) collective-permute-start(bf16[1,1,16,512]{3,2,1,0:T(8,128)(2,1)S(1)} %get-tuple-element.237), channel_id=1, source_target_pairs={{0,6},{1,7},{2,4},{3,5},{4,2},{5,3},{6,0},{7,1},{8,14},{9,15},{10,... | collective-permute-start | bytes 49160 | tf_op jit(solution)/shard_map/while/body/eval_jaxpr/ppermute | solution.py:22
  82.4 6.5 %collective-permute-start.6 = (bf16[1,1,16,512]{3,2,1,0:T(8,128)(2,1)S(1)}, bf16[1,1,16,512]{3,2,1,0:T(8,128)(2,1)S(1)}, u32[]{:S(2)}, u32[]{:S(2)}) collective-permute-start(bf16[1,1,16,512]{3,2,1,0:T(8,128)(2,1)S(1)} %get-tuple-element.238), channel_id=1, source_target_pairs={{0,7},{1,6},{2,5},{3,4},{4,3},{5,2},{6,1},{7,0},{8,15},{9,14},{10,... | collective-permute-start | bytes 49160 | tf_op jit(solution)/shard_map/while/body/eval_jaxpr/ppermute | solution.py:22
  82.7 9.6 %collective-permute-start.7 = (bf16[1,1,16,512]{3,2,1,0:T(8,128)(2,1)S(1)}, bf16[1,1,16,512]{3,2,1,0:T(8,128)(2,1)S(1)}, u32[]{:S(2)}, u32[]{:S(2)}) collective-permute-start(bf16[1,1,16,512]{3,2,1,0:T(8,128)(2,1)S(1)} %get-tuple-element.239), channel_id=1, source_target_pairs={{0,8},{1,9},{2,10},{3,11},{4,12},{5,13},{6,14},{7,15},{8,0},{9,1},... | collective-permute-start | bytes 49160 | tf_op jit(solution)/shard_map/while/body/eval_jaxpr/ppermute | solution.py:22
  85.1 7.3 %collective-permute-start.8 = (bf16[1,1,16,512]{3,2,1,0:T(8,128)(2,1)S(1)}, bf16[1,1,16,512]{3,2,1,0:T(8,128)(2,1)S(1)}, u32[]{:S(2)}, u32[]{:S(2)}) collective-permute-start(bf16[1,1,16,512]{3,2,1,0:T(8,128)(2,1)S(1)} %get-tuple-element.240), channel_id=1, source_target_pairs={{0,9},{1,8},{2,11},{3,10},{4,13},{5,12},{6,15},{7,14},{8,1},{9,0},... | collective-permute-start | bytes 49160 | tf_op jit(solution)/shard_map/while/body/eval_jaxpr/ppermute | solution.py:22
  85.3 11.4 %collective-permute-start.9 = (bf16[1,1,16,512]{3,2,1,0:T(8,128)(2,1)S(1)}, bf16[1,1,16,512]{3,2,1,0:T(8,128)(2,1)S(1)}, u32[]{:S(2)}, u32[]{:S(2)}) collective-permute-start(bf16[1,1,16,512]{3,2,1,0:T(8,128)(2,1)S(1)} %get-tuple-element.241), channel_id=1, source_target_pairs={{0,10},{1,11},{2,8},{3,9},{4,14},{5,15},{6,12},{7,13},{8,2},{9,3},... | collective-permute-start | bytes 49160 | tf_op jit(solution)/shard_map/while/body/eval_jaxpr/ppermute | solution.py:22
  88.6 8.3 %collective-permute-start.10 = (bf16[1,1,16,512]{3,2,1,0:T(8,128)(2,1)S(1)}, bf16[1,1,16,512]{3,2,1,0:T(8,128)(2,1)S(1)}, u32[]{:S(2)}, u32[]{:S(2)}) collective-permute-start(bf16[1,1,16,512]{3,2,1,0:T(8,128)(2,1)S(1)} %get-tuple-element.242), channel_id=1, source_target_pairs={{0,11},{1,10},{2,9},{3,8},{4,15},{5,14},{6,13},{7,12},{8,3},{9,2},... | collective-permute-start | bytes 49160 | tf_op jit(solution)/shard_map/while/body/eval_jaxpr/ppermute | solution.py:22
  88.9 8.0 %collective-permute-start.11 = (bf16[1,1,16,512]{3,2,1,0:T(8,128)(2,1)S(1)}, bf16[1,1,16,512]{3,2,1,0:T(8,128)(2,1)S(1)}, u32[]{:S(2)}, u32[]{:S(2)}) collective-permute-start(bf16[1,1,16,512]{3,2,1,0:T(8,128)(2,1)S(1)} %get-tuple-element.243), channel_id=1, source_target_pairs={{0,12},{1,13},{2,14},{3,15},{4,8},{5,9},{6,10},{7,11},{8,4},{9,5},... | collective-permute-start | bytes 49160 | tf_op jit(solution)/shard_map/while/body/eval_jaxpr/ppermute | solution.py:22
  92.2 5.0 %collective-permute-start.12 = (bf16[1,1,16,512]{3,2,1,0:T(8,128)(2,1)S(1)}, bf16[1,1,16,512]{3,2,1,0:T(8,128)(2,1)S(1)}, u32[]{:S(2)}, u32[]{:S(2)}) collective-permute-start(bf16[1,1,16,512]{3,2,1,0:T(8,128)(2,1)S(1)} %get-tuple-element.244), channel_id=1, source_target_pairs={{0,13},{1,12},{2,15},{3,14},{4,9},{5,8},{6,11},{7,10},{8,5},{9,4},... | collective-permute-start | bytes 49160 | tf_op jit(solution)/shard_map/while/body/eval_jaxpr/ppermute | solution.py:22
  92.4 6.4 %collective-permute-start.13 = (bf16[1,1,16,512]{3,2,1,0:T(8,128)(2,1)S(1)}, bf16[1,1,16,512]{3,2,1,0:T(8,128)(2,1)S(1)}, u32[]{:S(2)}, u32[]{:S(2)}) collective-permute-start(bf16[1,1,16,512]{3,2,1,0:T(8,128)(2,1)S(1)} %get-tuple-element.245), channel_id=1, source_target_pairs={{0,14},{1,15},{2,12},{3,13},{4,10},{5,11},{6,8},{7,9},{8,6},{9,7},... | collective-permute-start | bytes 49160 | tf_op jit(solution)/shard_map/while/body/eval_jaxpr/ppermute | solution.py:22
  96.7 5.9 %collective-permute-start.14 = (bf16[1,1,16,512]{3,2,1,0:T(8,128)(2,1)S(1)}, bf16[1,1,16,512]{3,2,1,0:T(8,128)(2,1)S(1)}, u32[]{:S(2)}, u32[]{:S(2)}) collective-permute-start(bf16[1,1,16,512]{3,2,1,0:T(8,128)(2,1)S(1)} %get-tuple-element.246), channel_id=1, source_target_pairs={{0,15},{1,14},{2,13},{3,12},{4,11},{5,10},{6,9},{7,8},{8,7},{9,6},... | collective-permute-start | bytes 49160 | tf_op jit(solution)/shard_map/while/body/eval_jaxpr/ppermute | solution.py:22
  104.9 22.9 %all-reduce.2.cloned.1.call-start = ((), (), s32[]{:S(2)}) async-start(), calls=%async_computation.2 | async-start | bytes 524288 | tf_op jit(solution)/shard_map/while/body/eval_jaxpr/psum | solution.py:34
  129.4 6.1 %collective-permute-start.1 = (bf16[1,1,16,512]{3,2,1,0:T(8,128)(2,1)S(1)}, bf16[1,1,16,512]{3,2,1,0:T(8,128)(2,1)S(1)}, u32[]{:S(2)}, u32[]{:S(2)}) collective-permute-start(bf16[1,1,16,512]{3,2,1,0:T(8,128)(2,1)S(1)} %get-tuple-element.233), channel_id=1, source_target_pairs={{0,2},{1,3},{2,0},{3,1},{4,6},{5,7},{6,4},{7,5},{8,10},{9,11},{10,... | collective-permute-start | bytes 49160 | tf_op jit(solution)/shard_map/while/body/eval_jaxpr/ppermute | solution.py:22
  131.0 4.9 %collective-permute-start.2 = (bf16[1,1,16,512]{3,2,1,0:T(8,128)(2,1)S(1)}, bf16[1,1,16,512]{3,2,1,0:T(8,128)(2,1)S(1)}, u32[]{:S(2)}, u32[]{:S(2)}) collective-permute-start(bf16[1,1,16,512]{3,2,1,0:T(8,128)(2,1)S(1)} %get-tuple-element.234), channel_id=1, source_target_pairs={{0,3},{1,2},{2,1},{3,0},{4,7},{5,6},{6,5},{7,4},{8,11},{9,10},{10,... | collective-permute-start | bytes 49160 | tf_op jit(solution)/shard_map/while/body/eval_jaxpr/ppermute | solution.py:22
  131.3 6.9 %collective-permute-start.3 = (bf16[1,1,16,512]{3,2,1,0:T(8,128)(2,1)S(1)}, bf16[1,1,16,512]{3,2,1,0:T(8,128)(2,1)S(1)}, u32[]{:S(2)}, u32[]{:S(2)}) collective-permute-start(bf16[1,1,16,512]{3,2,1,0:T(8,128)(2,1)S(1)} %get-tuple-element.235), channel_id=1, source_target_pairs={{0,4},{1,5},{2,6},{3,7},{4,0},{5,1},{6,2},{7,3},{8,12},{9,13},{10,... | collective-permute-start | bytes 49160 | tf_op jit(solution)/shard_map/while/body/eval_jaxpr/ppermute | solution.py:22
  132.8 5.7 %collective-permute-start.4 = (bf16[1,1,16,512]{3,2,1,0:T(8,128)(2,1)S(1)}, bf16[1,1,16,512]{3,2,1,0:T(8,128)(2,1)S(1)}, u32[]{:S(2)}, u32[]{:S(2)}) collective-permute-start(bf16[1,1,16,512]{3,2,1,0:T(8,128)(2,1)S(1)} %get-tuple-element.236), channel_id=1, source_target_pairs={{0,5},{1,4},{2,7},{3,6},{4,1},{5,0},{6,3},{7,2},{8,13},{9,12},{10,... | collective-permute-start | bytes 49160 | tf_op jit(solution)/shard_map/while/body/eval_jaxpr/ppermute | solution.py:22
  133.0 8.7 %collective-permute-start.5 = (bf16[1,1,16,512]{3,2,1,0:T(8,128)(2,1)S(1)}, bf16[1,1,16,512]{3,2,1,0:T(8,128)(2,1)S(1)}, u32[]{:S(2)}, u32[]{:S(2)}) collective-permute-start(bf16[1,1,16,512]{3,2,1,0:T(8,128)(2,1)S(1)} %get-tuple-element.237), channel_id=1, source_target_pairs={{0,6},{1,7},{2,4},{3,5},{4,2},{5,3},{6,0},{7,1},{8,14},{9,15},{10,... | collective-permute-start | bytes 49160 | tf_op jit(solution)/shard_map/while/body/eval_jaxpr/ppermute | solution.py:22
  135.5 6.5 %collective-permute-start.6 = (bf16[1,1,16,512]{3,2,1,0:T(8,128)(2,1)S(1)}, bf16[1,1,16,512]{3,2,1,0:T(8,128)(2,1)S(1)}, u32[]{:S(2)}, u32[]{:S(2)}) collective-permute-start(bf16[1,1,16,512]{3,2,1,0:T(8,128)(2,1)S(1)} %get-tuple-element.238), channel_id=1, source_target_pairs={{0,7},{1,6},{2,5},{3,4},{4,3},{5,2},{6,1},{7,0},{8,15},{9,14},{10,... | collective-permute-start | bytes 49160 | tf_op jit(solution)/shard_map/while/body/eval_jaxpr/ppermute | solution.py:22
  135.8 9.6 %collective-permute-start.7 = (bf16[1,1,16,512]{3,2,1,0:T(8,128)(2,1)S(1)}, bf16[1,1,16,512]{3,2,1,0:T(8,128)(2,1)S(1)}, u32[]{:S(2)}, u32[]{:S(2)}) collective-permute-start(bf16[1,1,16,512]{3,2,1,0:T(8,128)(2,1)S(1)} %get-tuple-element.239), channel_id=1, source_target_pairs={{0,8},{1,9},{2,10},{3,11},{4,12},{5,13},{6,14},{7,15},{8,0},{9,1},... | collective-permute-start | bytes 49160 | tf_op jit(solution)/shard_map/while/body/eval_jaxpr/ppermute | solution.py:22
  138.2 7.3 %collective-permute-start.8 = (bf16[1,1,16,512]{3,2,1,0:T(8,128)(2,1)S(1)}, bf16[1,1,16,512]{3,2,1,0:T(8,128)(2,1)S(1)}, u32[]{:S(2)}, u32[]{:S(2)}) collective-permute-start(bf16[1,1,16,512]{3,2,1,0:T(8,128)(2,1)S(1)} %get-tuple-element.240), channel_id=1, source_target_pairs={{0,9},{1,8},{2,11},{3,10},{4,13},{5,12},{6,15},{7,14},{8,1},{9,0},... | collective-permute-start | bytes 49160 | tf_op jit(solution)/shard_map/while/body/eval_jaxpr/ppermute | solution.py:22
  138.4 11.4 %collective-permute-start.9 = (bf16[1,1,16,512]{3,2,1,0:T(8,128)(2,1)S(1)}, bf16[1,1,16,512]{3,2,1,0:T(8,128)(2,1)S(1)}, u32[]{:S(2)}, u32[]{:S(2)}) collective-permute-start(bf16[1,1,16,512]{3,2,1,0:T(8,128)(2,1)S(1)} %get-tuple-element.241), channel_id=1, source_target_pairs={{0,10},{1,11},{2,8},{3,9},{4,14},{5,15},{6,12},{7,13},{8,2},{9,3},... | collective-permute-start | bytes 49160 | tf_op jit(solution)/shard_map/while/body/eval_jaxpr/ppermute | solution.py:22
  141.7 8.3 %collective-permute-start.10 = (bf16[1,1,16,512]{3,2,1,0:T(8,128)(2,1)S(1)}, bf16[1,1,16,512]{3,2,1,0:T(8,128)(2,1)S(1)}, u32[]{:S(2)}, u32[]{:S(2)}) collective-permute-start(bf16[1,1,16,512]{3,2,1,0:T(8,128)(2,1)S(1)} %get-tuple-element.242), channel_id=1, source_target_pairs={{0,11},{1,10},{2,9},{3,8},{4,15},{5,14},{6,13},{7,12},{8,3},{9,2},... | collective-permute-start | bytes 49160 | tf_op jit(solution)/shard_map/while/body/eval_jaxpr/ppermute | solution.py:22
  142.0 8.0 %collective-permute-start.11 = (bf16[1,1,16,512]{3,2,1,0:T(8,128)(2,1)S(1)}, bf16[1,1,16,512]{3,2,1,0:T(8,128)(2,1)S(1)}, u32[]{:S(2)}, u32[]{:S(2)}) collective-permute-start(bf16[1,1,16,512]{3,2,1,0:T(8,128)(2,1)S(1)} %get-tuple-element.243), channel_id=1, source_target_pairs={{0,12},{1,13},{2,14},{3,15},{4,8},{5,9},{6,10},{7,11},{8,4},{9,5},... | collective-permute-start | bytes 49160 | tf_op jit(solution)/shard_map/while/body/eval_jaxpr/ppermute | solution.py:22
  145.4 5.0 %collective-permute-start.12 = (bf16[1,1,16,512]{3,2,1,0:T(8,128)(2,1)S(1)}, bf16[1,1,16,512]{3,2,1,0:T(8,128)(2,1)S(1)}, u32[]{:S(2)}, u32[]{:S(2)}) collective-permute-start(bf16[1,1,16,512]{3,2,1,0:T(8,128)(2,1)S(1)} %get-tuple-element.244), channel_id=1, source_target_pairs={{0,13},{1,12},{2,15},{3,14},{4,9},{5,8},{6,11},{7,10},{8,5},{9,4},... | collective-permute-start | bytes 49160 | tf_op jit(solution)/shard_map/while/body/eval_jaxpr/ppermute | solution.py:22
  145.5 6.4 %collective-permute-start.13 = (bf16[1,1,16,512]{3,2,1,0:T(8,128)(2,1)S(1)}, bf16[1,1,16,512]{3,2,1,0:T(8,128)(2,1)S(1)}, u32[]{:S(2)}, u32[]{:S(2)}) collective-permute-start(bf16[1,1,16,512]{3,2,1,0:T(8,128)(2,1)S(1)} %get-tuple-element.245), channel_id=1, source_target_pairs={{0,14},{1,15},{2,12},{3,13},{4,10},{5,11},{6,8},{7,9},{8,6},{9,7},... | collective-permute-start | bytes 49160 | tf_op jit(solution)/shard_map/while/body/eval_jaxpr/ppermute | solution.py:22
  149.8 5.9 %collective-permute-start.14 = (bf16[1,1,16,512]{3,2,1,0:T(8,128)(2,1)S(1)}, bf16[1,1,16,512]{3,2,1,0:T(8,128)(2,1)S(1)}, u32[]{:S(2)}, u32[]{:S(2)}) collective-permute-start(bf16[1,1,16,512]{3,2,1,0:T(8,128)(2,1)S(1)} %get-tuple-element.246), channel_id=1, source_target_pairs={{0,15},{1,14},{2,13},{3,12},{4,11},{5,10},{6,9},{7,8},{8,7},{9,6},... | collective-permute-start | bytes 49160 | tf_op jit(solution)/shard_map/while/body/eval_jaxpr/ppermute | solution.py:22
  158.1 13.7 %reduce-scatter.2.cloned.1.call-start = ((), (), s32[]{:S(2)}) async-start(), calls=%async_computation.1 | async-start | bytes 786432 | tf_op jit(solution)/shard_map/reduce_scatter | solution.py:89
  (8 other events, 32.1 us)
Sparse Core Ops, SparseCore 0:
  48.8 25.8 all-reduce.1
  108.1 19.6 all-reduce.1
Sparse Core Ops, SparseCore 1:
  160.8 10.9 reduce-scatter.1
